TPU v7x, 32 devices: a whole 2x2x4 slice. The times are simulated.
32 devices in a mesh: tx: 4 (over y, x), ty: 8 (over z, core).
Axes of the slice: x: 2, y: 2, z: 4, core: 2. Of those that a mesh axis runs over, the one named last changes fastest.
Arguments:
- stack: bfloat16 [32, 2, 128, 4096], P('tx', None, None, 'ty'), may hold values from -6 to 6
- filt_re: bfloat16 [32, 32], replicated, may hold values from -0.75 to 0.75
- filt_im: bfloat16 [32, 32], replicated, may hold values from -0.75 to 0.75
- pre_ids: int32 [32], replicated, may hold values from 0 to 15
- post_ids: int32 [32], replicated, may hold values from 16 to 31
Outputs:
- coherence: float32 [32, 128, 4096], P(None, 'ty', 'tx')
- change: float32 [32, 128, 4096], P(None, 'ty', 'tx')
All inputs are finite; a program needn't handle non-finite values.
Results may differ from a plain program's by a relative error of at most 0.0065.
Values may be sent and summed in bfloat16 or wider, within the bound.
No kernel may reach another device: no remote copies, remote signals or barrier semaphores. Data moves between devices by JAX's collectives and lax.ppermute only.
A program may use at most 128 MiB of HBM per device.

v0:
```python
import jax
import jax.numpy as jnp
from jax import lax
from jax.sharding import PartitionSpec as P

RADIUS = 4


def with_halo(block, sides, width):
    for axis, dim in sides:
        count = lax.axis_size(axis)
        forward = [(i, i + 1) for i in range(count - 1)]
        backward = [(target, source) for source, target in forward]
        low = lax.ppermute(
            lax.slice_in_dim(block, block.shape[dim] - width, None, axis=dim), axis, forward
        )
        high = lax.ppermute(lax.slice_in_dim(block, 0, width, axis=dim), axis, backward)
        block = jnp.concatenate([low, block, high], axis=dim)
    return block


def box_mean(fields, tile_rows, tile_cols, radius):
    window = 2 * radius + 1
    out_rows = jnp.arange(tile_rows)[:, None]
    in_rows = jnp.arange(tile_rows + 2 * radius)[None, :]
    row_gap = in_rows - out_rows
    row_band = jnp.where((row_gap >= 0) & (row_gap <= 2 * radius), 1.0, 0.0).astype(jnp.float32)
    in_cols = jnp.arange(tile_cols + 2 * radius)[:, None]
    out_cols = jnp.arange(tile_cols)[None, :]
    col_gap = in_cols - out_cols
    col_band = jnp.where((col_gap >= 0) & (col_gap <= 2 * radius), 1.0, 0.0).astype(jnp.float32)
    rowsum = jnp.einsum("ij,fjw->fiw", row_band, fields, precision=lax.Precision.HIGHEST)
    colsum = jnp.einsum("fiw,wk->fik", rowsum, col_band, precision=lax.Precision.HIGHEST)
    return colsum / float(window * window)


def pair_maps(padded, pre_ids, post_ids, tile_rows, tile_cols, radius):
    widened = padded.astype(jnp.float32)
    power = widened[:, 0] * widened[:, 0] + widened[:, 1] * widened[:, 1]
    pre_side = jnp.take(widened, pre_ids, axis=0)
    post_side = jnp.take(widened, post_ids, axis=0)
    cross_re = pre_side[:, 0] * post_side[:, 0] + pre_side[:, 1] * post_side[:, 1]
    cross_im = pre_side[:, 1] * post_side[:, 0] - pre_side[:, 0] * post_side[:, 1]
    fields = jnp.concatenate([power, cross_re, cross_im], axis=0)
    means = box_mean(fields, tile_rows, tile_cols, radius)
    count_acq = power.shape[0]
    count_pairs = pre_ids.shape[0]
    power_mean = means[:count_acq] + 1e-06
    pre_power = jnp.take(power_mean, pre_ids, axis=0)
    post_power = jnp.take(power_mean, post_ids, axis=0)
    real_mean = means[count_acq : count_acq + count_pairs]
    imag_mean = means[count_acq + count_pairs :]
    coherence = jnp.sqrt(real_mean * real_mean + imag_mean * imag_mean) / jnp.sqrt(
        pre_power * post_power
    )
    change = jnp.log(post_power / pre_power)
    return (coherence, change)


def shards(stack, filt_re, filt_im, pre_ids, post_ids):
    count_acq = filt_re.shape[0]
    mixing = jnp.stack([jnp.stack([filt_re, -filt_im], -1), jnp.stack([filt_im, filt_re], -1)], 1)
    mixing = mixing.reshape(2 * count_acq, 2 * count_acq)
    n_rows = lax.axis_size("ty")
    n_cols = lax.axis_size("tx")
    tile_rows = stack.shape[2] // n_rows
    tile_cols = stack.shape[3] * n_rows // n_cols
    by_rows = lax.all_to_all(stack, "ty", split_axis=2, concat_axis=3, tiled=True)
    piece = lax.all_to_all(by_rows, "tx", split_axis=3, concat_axis=0, tiled=True)
    height = piece.shape[2]
    breadth = piece.shape[3]
    flat = piece.reshape(2 * count_acq, height * breadth)
    result = jnp.dot(mixing, flat, preferred_element_type=jnp.float32)
    filtered = result.astype(jnp.bfloat16).reshape(count_acq, 2, height, breadth)
    padded = with_halo(filtered, (("tx", 3), ("ty", 2)), RADIUS)
    return pair_maps(padded, pre_ids, post_ids, tile_rows, tile_cols, RADIUS)


def solution(mesh):
    in_specs = (P("tx", None, None, "ty"), P(), P(), P(), P())
    out_specs = (P(None, "ty", "tx"), P(None, "ty", "tx"))
    return jax.shard_map(shards, mesh=mesh, in_specs=in_specs, out_specs=out_specs, check_vma=False)
```

profile of v0, /device:TPU:21, one launch (start us, length us, event | category | flops | bytes accessed | tf_op | source)
XLA Modules:
  0.0 292.3 jit_solution(7428069221730173030)
XLA Ops:
  0.6 2.8 copy.47
  3.4 50.5 %all_to_all.33 = bf16[8,2,128,512]{3,0,1,2:T(8,128)(2,1)S(1)} all-to-all(bf16[8,2,128,512]{3,0,1,2:T(8,128)(2,1)S(1)} %copy.47), channel_id=1, replica_groups=mesh['tx'=4,'ty'=8] {'ty'}, dimensions={2} | all-to-all | bytes 4194304 | tf_op jit(solution)/shard_map/all_to_all | solution.py:68
  53.9 20.2 %copy.58 = bf16[8,2,16,8,512]{2,1,0,4,3:T(2,128)(2,1)} copy(bf16[8,2,16,8,512]{4,0,1,2,3:T(8,128)(2,1)S(1)} %bitcast.50) | data formatting | bytes 4194304 | tf_op jit(solution)/shard_map/all_to_all | solution.py:68
  74.1 20.3 %reshape.82 = bf16[4,2,131072]{2,1,0:T(2,128)(2,1)} reshape(bf16[4096,8,2,16]{3,2,1,0:T(2,128)(2,1)} %bitcast.46) | data formatting | bytes 4194304
  94.4 3.9 %all-to-all-start.1 = ((bf16[4,2,131072]{2,1,0:T(2,128)(2,1)}), bf16[4,2,131072]{2,1,0:T(2,128)(2,1)S(1)}, u32[]{:S(2)}, u32[]{:S(2)}) async-start(bf16[4,2,131072]{2,1,0:T(2,128)(2,1)} %reshape.82), calls=%async_computation.1 | async-start | bytes 4194304 | tf_op jit(solution)/shard_map/all_to_all | solution.py:69
  99.8 22.2 %all-to-all-done.1 = bf16[4,2,131072]{2,1,0:T(2,128)(2,1)S(1)} async-done(((bf16[4,2,131072]{2,1,0:T(2,128)(2,1)}), bf16[4,2,131072]{2,1,0:T(2,128)(2,1)S(1)}, u32[]{:S(2)}, u32[]{:S(2)}) %all-to-all-start.1) | async-done | bytes 2097184 | tf_op jit(solution)/shard_map/all_to_all | solution.py:69
  122.0 13.4 %reshape.83 = bf16[4096,8,2,16]{3,2,1,0:T(2,128)(2,1)} reshape(bf16[4,2,131072]{2,1,0:T(2,128)(2,1)S(1)} %all-to-all-done.1) | data formatting | bytes 4194304
  135.4 35.3 %copy.50 = bf16[8,2,16,4,1024]{4,2,1,0,3:T(8,128)(2,1)S(1)} copy(bf16[8,2,16,4,1024]{2,1,0,4,3:T(2,128)(2,1)} %bitcast.47) | data formatting | bytes 4194304 | tf_op jit(solution)/shard_map/all_to_all | solution.py:69
  174.0 3.0 %collective-permute-start.1 = (bf16[32,2,16,4]{3,2,0,1:T(8,128)(2,1)S(1)}, bf16[32,2,16,4]{3,2,0,1:T(8,128)(2,1)S(1)}, u32[]{:S(2)}, u32[]{:S(2)}) collective-permute-start(bf16[32,2,16,4]{3,2,0,1:T(8,128)(2,1)S(1)} %get-tuple-element.10), channel_id=1, source_target_pairs={{8,0},{16,8},{24,16},{9,1},{17,9},{25,17},{10,2},{18,10},{26,18},{... | collective-permute-start | bytes 24584 | tf_op jit(solution)/shard_map/ppermute | solution.py:17
  177.0 2.3 collective-permute-start
  181.8 6.5 %collective-permute-done = bf16[32,2,16,4]{3,2,0,1:T(8,128)(2,1)S(1)} collective-permute-done((bf16[32,2,16,4]{3,2,0,1:T(8,128)(2,1)S(1)}, bf16[32,2,16,4]{3,2,0,1:T(8,128)(2,1)S(1)}, u32[]{:S(2)}, u32[]{:S(2)}) %collective-permute-start) | collective-permute-done | bytes 8224 | tf_op jit(solution)/shard_map/ppermute | solution.py:14
  188.3 4.8 %concatenate.9 = bf16[32,2,16,1032]{3,2,0,1:T(8,128)(2,1)S(1)} concatenate(bf16[32,2,16,4]{3,2,0,1:T(8,128)(2,1)S(1)} %collective-permute-done, bf16[32,2,16,1024]{3,2,0,1:T(8,128)(2,1)} %copy.51, bf16[32,2,16,4]{3,2,0,1:T(8,128)(2,1)S(1)} %collective-permute-done.1), dimensions={3} | concatenate | bytes 4227072 | tf_op jit(solution)/shard_map/concatenate | solution.py:18
  193.6 6.8 %collective-permute-start.2 = (bf16[32,2,4,1032]{3,2,0,1:T(4,128)(2,1)S(1)}, bf16[32,2,4,1032]{3,2,0,1:T(4,128)(2,1)S(1)}, u32[]{:S(2)}, u32[]{:S(2)}) collective-permute-start(bf16[32,2,4,1032]{3,2,0,1:T(4,128)(2,1)S(1)} %get-tuple-element.8), channel_id=1, source_target_pairs={{0,1},{1,2},{2,3},{3,4},{4,5},{5,6},{6,7},{8,9},{9,10},{10,11},{11... | collective-permute-start | bytes 1585160 | tf_op jit(solution)/shard_map/ppermute | solution.py:14
  202.5 4.6 %collective-permute-done.2 = bf16[32,2,4,1032]{3,2,0,1:T(4,128)(2,1)S(1)} collective-permute-done((bf16[32,2,4,1032]{3,2,0,1:T(4,128)(2,1)S(1)}, bf16[32,2,4,1032]{3,2,0,1:T(4,128)(2,1)S(1)}, u32[]{:S(2)}, u32[]{:S(2)}) %collective-permute-start.2) | collective-permute-done | bytes 528416 | tf_op jit(solution)/shard_map/ppermute | solution.py:14
  207.1 4.4 %collective-permute-done.3 = bf16[32,2,4,1032]{3,2,0,1:T(4,128)(2,1)S(1)} collective-permute-done((bf16[32,2,4,1032]{3,2,0,1:T(4,128)(2,1)S(1)}, bf16[32,2,4,1032]{3,2,0,1:T(4,128)(2,1)S(1)}, u32[]{:S(2)}, u32[]{:S(2)}) %collective-permute-start.3) | collective-permute-done | bytes 528416 | tf_op jit(solution)/shard_map/ppermute | solution.py:17
  215.3 3.4 %copy.54 = f32[32,2,24,1032]{3,2,1,0:T(8,128)} copy(f32[32,2,24,1032]{3,2,0,1:T(8,128)S(1)} %maximum_convert_fusion) | data formatting | bytes 12681216 | tf_op jit(solution)/shard_map/convert_element_type | solution.py:38
  218.7 7.0 %gather_fusion.1 = f32[32,2,24,1032]{3,2,1,0:T(8,128)} fusion(f32[32,2,24,1032]{3,2,1,0:T(8,128)} %copy.54, s32[1024]{0:T(1024)S(1)} %pad_clamp_fusion), kind=kCustom, calls=%fused_computation.2.clone | custom fusion | bytes 12681344 | tf_op jit(solution)/shard_map/jit(_take)/gather | solution.py:41
  225.7 6.8 %gather_fusion = f32[32,2,24,1032]{3,2,1,0:T(8,128)} fusion(f32[32,2,24,1032]{3,2,1,0:T(8,128)} %copy.54, s32[1024]{0:T(1024)S(1)} %pad_clamp_fusion.1), kind=kCustom, calls=%fused_computation.clone | custom fusion | bytes 12681344 | tf_op jit(solution)/shard_map/jit(_take)/gather | solution.py:40
  232.5 5.7 %copy_select_fusion = (f32[32,2,24,1032]{3,2,0,1:T(8,128)S(1)}, f32[32,2,24,1032]{3,2,0,1:T(8,128)S(1)}) fusion(f32[32,2,24,1032]{3,2,1,0:T(8,128)} %gather_fusion.1, pred[32]{0:T(512)(128)(4,1)S(1)} %compare_and_fusion, f32[32,2,24,1032]{3,2,1,0:T(8,128)} %gather_fusion, pred[32]{0:T(512)(128)(4,1)S(1)} %compare_and_fusion.1), kind=kLoop, calls=%fused_computation.13 | loop fusion | flops 3170304 | bytes 25362496 | tf_op jit(solution)/shard_map/jit(_take)/select_n | solution.py:41
  238.2 3.6 %add_bitcast_fusion = (f32[32,24,1032]{2,1,0:T(8,128)}, f32[32,24,1032]{2,1,0:T(8,128)}) fusion(f32[32,2,24,1032]{3,2,0,1:T(8,128)S(1)} %get-tuple-element.14, f32[32,2,24,1032]{3,2,0,1:T(8,128)S(1)} %get-tuple-element.15), kind=kLoop, calls=%fused_computation.27 | loop fusion | flops 4755456 | bytes 19021824 | tf_op jit(solution)/shard_map/add | solution.py:42
  241.8 9.5 %fusion = f32[96,1032,16]{1,2,0:T(8,128)S(1)} fusion(f32[32,24,1032]{2,1,0:T(8,128)} %get-tuple-element.5, f32[32,24,1032]{2,1,0:T(8,128)} %get-tuple-element.4, f32[32,24,1032]{2,1,0:T(8,128)} %fusion.16), kind=kOutput, calls=%fused_computation.5 | convolution fusion | flops 461281152 | bytes 15851520 | tf_op jit(solution)/shard_map/ij,fjw->fiw/dot_general | solution.py:32
  251.4 26.9 %broadcast_multiply_fusion = f32[96,16,1024]{2,1,0:T(8,128)S(1)} fusion(f32[96,1032,16]{1,2,0:T(8,128)S(1)} %fusion), kind=kOutput, calls=%fused_computation.28 | convolution fusion | flops 19485204480 | bytes 12632064 | tf_op jit(solution)/shard_map/fiw,wk->fik/dot_general | solution.py:33
  278.3 2.7 copy-done
  285.1 7.1 %divide_log_fusion = (f32[32,16,1024]{2,1,0:T(8,128)}, f32[32,16,1024]{2,1,0:T(8,128)}) fusion(f32[32,16,1024]{2,1,0:T(8,128)} %gather_fusion.3, f32[32,16,1024]{2,1,0:T(8,128)} %gather_fusion.2, pred[32]{0:T(512)(128)(4,1)S(1)} %compare_and_fusion, pred[32]{0:T(512)(128)(4,1)S(1)} %compare_and_fusion.1, f32[96,16,1024]{2,1,0:T(8,128)} %copy-done), kind=kLoop, calls=%fused_computation.39 | loop fusion | flops 4194304 | bytes 12582976 | tf_op jit(solution)/shard_map/log | solution.py:56
  (33 shorter events, 17.7 us)
Async XLA Ops:
  94.4 4.0 %copy-start.1 = (bf16[32,32]{1,0:T(8,128)(2,1)S(1)}, bf16[32,32]{1,0:T(8,128)(2,1)}, u32[]{:S(2)}) copy-start(bf16[32,32]{1,0:T(8,128)(2,1)} %param.11) | copy-start | bytes 6148
  94.4 4.0 %copy-start.2 = (bf16[32,32]{1,0:T(8,128)(2,1)S(1)}, bf16[32,32]{1,0:T(8,128)(2,1)}, u32[]{:S(2)}) copy-start(bf16[32,32]{1,0:T(8,128)(2,1)} %param.10) | copy-start | bytes 6148
  94.4 5.3 %copy-start.3 = (s32[32]{0:T(128)S(1)}, s32[32]{0:T(128)}, u32[]{:S(2)}) copy-start(s32[32]{0:T(128)} %param.12) | copy-start | bytes 388
  94.4 5.3 %copy-start.4 = (s32[32]{0:T(128)S(1)}, s32[32]{0:T(128)}, u32[]{:S(2)}) copy-start(s32[32]{0:T(128)} %param.13) | copy-start | bytes 388
  94.4 27.6 %all-to-all-start.1 = ((bf16[4,2,131072]{2,1,0:T(2,128)(2,1)}), bf16[4,2,131072]{2,1,0:T(2,128)(2,1)S(1)}, u32[]{:S(2)}, u32[]{:S(2)}) async-start(bf16[4,2,131072]{2,1,0:T(2,128)(2,1)} %reshape.82), calls=%async_computation.1 | async-start | bytes 4194304 | tf_op jit(solution)/shard_map/all_to_all | solution.py:69
  174.0 7.7 %collective-permute-start.1 = (bf16[32,2,16,4]{3,2,0,1:T(8,128)(2,1)S(1)}, bf16[32,2,16,4]{3,2,0,1:T(8,128)(2,1)S(1)}, u32[]{:S(2)}, u32[]{:S(2)}) collective-permute-start(bf16[32,2,16,4]{3,2,0,1:T(8,128)(2,1)S(1)} %get-tuple-element.10), channel_id=1, source_target_pairs={{8,0},{16,8},{24,16},{9,1},{17,9},{25,17},{10,2},{18,10},{26,18},{... | collective-permute-start | bytes 24584 | tf_op jit(solution)/shard_map/ppermute | solution.py:17
  177.0 11.2 %collective-permute-start = (bf16[32,2,16,4]{3,2,0,1:T(8,128)(2,1)S(1)}, bf16[32,2,16,4]{3,2,0,1:T(8,128)(2,1)S(1)}, u32[]{:S(2)}, u32[]{:S(2)}) collective-permute-start(bf16[32,2,16,4]{3,2,0,1:T(8,128)(2,1)S(1)} %get-tuple-element.11), channel_id=1, source_target_pairs={{0,8},{8,16},{16,24},{1,9},{9,17},{17,25},{2,10},{10,18},{18,26},{... | collective-permute-start | bytes 24584 | tf_op jit(solution)/shard_map/ppermute | solution.py:14
  193.6 13.6 %collective-permute-start.2 = (bf16[32,2,4,1032]{3,2,0,1:T(4,128)(2,1)S(1)}, bf16[32,2,4,1032]{3,2,0,1:T(4,128)(2,1)S(1)}, u32[]{:S(2)}, u32[]{:S(2)}) collective-permute-start(bf16[32,2,4,1032]{3,2,0,1:T(4,128)(2,1)S(1)} %get-tuple-element.8), channel_id=1, source_target_pairs={{0,1},{1,2},{2,3},{3,4},{4,5},{5,6},{6,7},{8,9},{9,10},{10,11},{11... | collective-permute-start | bytes 1585160 | tf_op jit(solution)/shard_map/ppermute | solution.py:14
  200.3 11.2 %collective-permute-start.3 = (bf16[32,2,4,1032]{3,2,0,1:T(4,128)(2,1)S(1)}, bf16[32,2,4,1032]{3,2,0,1:T(4,128)(2,1)S(1)}, u32[]{:S(2)}, u32[]{:S(2)}) collective-permute-start(bf16[32,2,4,1032]{3,2,0,1:T(4,128)(2,1)S(1)} %get-tuple-element.9), channel_id=1, source_target_pairs={{1,0},{2,1},{3,2},{4,3},{5,4},{6,5},{7,6},{9,8},{10,9},{11,10},{12... | collective-permute-start | bytes 1585160 | tf_op jit(solution)/shard_map/ppermute | solution.py:17
  278.3 2.7 copy-start
where the time goes:
time: 293 us; the launch traced here: 292 us
  local copies, waits for them, and re-layouts  127 us (43%)
  blocking collectives  50.5 us (17%)
  waiting for transfers between devices  38.6 us (13%)
  matrix products  37.1 us (13%)
  other arithmetic  20.5 us (7%)
  starting transfers between devices  18.1 us (6%)
    all_to_all x1, blocking collectives, shards(): lax.all_to_all(stack, 'ty', split_axis=2, concat_axis=3, tiled=True)  50.5 us
    unnamed x15, local copies, waits for them, and re-layouts  41.6 us
    all_to_all x1, local copies, waits for them, and re-layouts, shards(): lax.all_to_all(by_rows, 'tx', split_axis=3, concat_axis=0, tiled=True)  35.3 us
    dot_general x1, matrix products, box_mean(): jnp.einsum('fiw,wk->fik', rowsum, col_band, precision=lax.Precision.HIGHEST)  26.9 us
    all_to_all x1, waiting for transfers between devices, shards(): lax.all_to_all(by_rows, 'tx', split_axis=3, concat_axis=0, tiled=True)  22.2 us
    all_to_all x1, local copies, waits for them, and re-layouts, shards(): lax.all_to_all(stack, 'ty', split_axis=2, concat_axis=3, tiled=True)  20.2 us
    ppermute x2, waiting for transfers between devices, with_halo(): lax.ppermute(lax.slice_in_dim(block, block.shape[dim] - width, None, axis...  11.1 us
    dot_general x1, matrix products, box_mean(): jnp.einsum('ij,fjw->fiw', row_band, fields, precision=lax.Precision.HIGHEST)  9.53 us
  transfers between devices with their start and end apart: 5, of which 5 were waited for; matrix products, arithmetic and copies ran while one was open for 1% of the time, Pallas kernels for 0%

commit v1 on v0

--- a/solution.py
+++ b/solution.py
@@ -66,7 +66,10 @@
     tile_rows = stack.shape[2] // n_rows
     tile_cols = stack.shape[3] * n_rows // n_cols
     by_rows = lax.all_to_all(stack, "ty", split_axis=2, concat_axis=3, tiled=True)
-    piece = lax.all_to_all(by_rows, "tx", split_axis=3, concat_axis=0, tiled=True)
+    piece = jnp.concatenate(
+        lax.all_to_all(jnp.stack(jnp.split(by_rows, lax.axis_size("tx"), axis=3)), "tx", 0, 0),
+        axis=0,
+    )
     height = piece.shape[2]
     breadth = piece.shape[3]
     flat = piece.reshape(2 * count_acq, height * breadth)

time: 293 us -> 211 us (0.72)
  local copies, waits for them, and re-layouts: 127 us -> 42.8 us
    all_to_all x1 -> x0, local copies, waits for them, and re-layouts: 35.3 us -> none  [shards(): lax.all_to_all(by_rows, 'tx', split_axis=3, concat_axis=0, tiled=True)]
    unnamed x15 -> x13, local copies, waits for them, and re-layouts: 41.6 us -> 7.85 us
    all_to_all x1 -> x2, local copies, waits for them, and re-layouts: 20.2 us -> 5.36 us  [shards(): lax.all_to_all(stack, 'ty', split_axis=2, concat_axis=3, tiled=True)]
where the time goes in v1:
time: 211 us; the launch traced here: 210 us
  blocking collectives  50.5 us (24%)
  local copies, waits for them, and re-layouts  42.8 us (20%)
  waiting for transfers between devices  38.7 us (18%)
  matrix products  37.1 us (18%)
  other arithmetic  22.1 us (10%)
  starting transfers between devices  18.1 us (9%)
    all_to_all x1, blocking collectives, shards(): lax.all_to_all(stack, 'ty', split_axis=2, concat_axis=3, tiled=True)  50.5 us
    dot_general x1, matrix products, box_mean(): jnp.einsum('fiw,wk->fik', rowsum, col_band, precision=lax.Precision.HIGHEST)  26.8 us
    all_to_all x1, waiting for transfers between devices, shards(): lax.all_to_all(jnp.stack(jnp.split(by_rows, lax.axis_size('tx'), axis=3))...  22.2 us
    ppermute x2, waiting for transfers between devices, with_halo(): lax.ppermute(lax.slice_in_dim(block, block.shape[dim] - width, None, axis...  11.1 us
    dot_general x1, matrix products, box_mean(): jnp.einsum('ij,fjw->fiw', row_band, fields, precision=lax.Precision.HIGHEST)  9.53 us
    ppermute x2, starting transfers between devices, with_halo(): lax.ppermute(lax.slice_in_dim(block, block.shape[dim] - width, None, axis...  9.06 us
    unnamed x13, local copies, waits for them, and re-layouts  7.85 us
    log x1, other arithmetic, pair_maps(): change = jnp.log(post_power / pre_power)  7.12 us
  transfers between devices with their start and end apart: 5, of which 5 were waited for; matrix products, arithmetic and copies ran while one was open for 1% of the time, Pallas kernels for 0%

profile of v1, /device:TPU:21, one launch (start us, length us, event | category | flops | bytes accessed | tf_op | source)
XLA Modules:
  0.0 210.1 jit_solution(862703232935006013)
XLA Ops:
  0.6 2.8 %copy.43 = bf16[8,2,128,512]{3,0,1,2:T(8,128)(2,1)S(1)} copy(bf16[8,2,128,512]{3,2,1,0:T(8,128)(2,1)} %param.9) | data formatting | bytes 4194304 | tf_op args[0]
  3.4 50.5 %all_to_all.23 = bf16[8,2,128,512]{3,0,1,2:T(8,128)(2,1)S(1)} all-to-all(bf16[8,2,128,512]{3,0,1,2:T(8,128)(2,1)S(1)} %copy.43), channel_id=1, replica_groups=mesh['tx'=4,'ty'=8] {'ty'}, dimensions={2} | all-to-all | bytes 4194304 | tf_op jit(solution)/shard_map/all_to_all | solution.py:68
  53.9 2.5 %copy.59 = bf16[8,2,8,16,512]{4,2,3,1,0:T(8,128)(2,1)} copy(bf16[8,2,8,16,512]{4,0,1,3,2:T(8,128)(2,1)S(1)} %bitcast.56) | data formatting | bytes 4194304 | tf_op jit(solution)/shard_map/all_to_all | solution.py:68
  56.4 2.9 %all_to_all.19 = bf16[8,2,16,4096]{3,2,1,0:T(8,128)(2,1)S(1)} reshape(bf16[8,2,16,8,512]{4,3,2,1,0:T(8,128)(2,1)} %bitcast.57) | data formatting | bytes 4194304 | tf_op jit(solution)/shard_map/all_to_all | solution.py:68
  61.0 3.9 %all-to-all-start.1 = ((bf16[4,8,2,16,1024]{4,3,2,1,0:T(8,128)(2,1)}), bf16[4,8,2,16,1024]{4,3,2,1,0:T(8,128)(2,1)S(1)}, u32[]{:S(2)}, u32[]{:S(2)}) async-start(bf16[4,8,2,16,1024]{4,3,2,1,0:T(8,128)(2,1)} %pad_maximum_fusion), calls=%async_computation.1 | async-start | bytes 4194304 | tf_op jit(solution)/shard_map/all_to_all | solution.py:70
  66.4 22.2 %all-to-all-done.1 = bf16[4,8,2,16,1024]{4,3,2,1,0:T(8,128)(2,1)S(1)} async-done(((bf16[4,8,2,16,1024]{4,3,2,1,0:T(8,128)(2,1)}), bf16[4,8,2,16,1024]{4,3,2,1,0:T(8,128)(2,1)S(1)}, u32[]{:S(2)}, u32[]{:S(2)}) %all-to-all-start.1) | async-done | bytes 2097184 | tf_op jit(solution)/shard_map/all_to_all | solution.py:70
  91.9 3.0 %collective-permute-start.1 = (bf16[32,2,16,4]{3,2,0,1:T(8,128)(2,1)S(1)}, bf16[32,2,16,4]{3,2,0,1:T(8,128)(2,1)S(1)}, u32[]{:S(2)}, u32[]{:S(2)}) collective-permute-start(bf16[32,2,16,4]{3,2,0,1:T(8,128)(2,1)S(1)} %get-tuple-element.10), channel_id=1, source_target_pairs={{8,0},{16,8},{24,16},{9,1},{17,9},{25,17},{10,2},{18,10},{26,18},{... | collective-permute-start | bytes 24584 | tf_op jit(solution)/shard_map/ppermute | solution.py:17
  94.9 2.3 %collective-permute-start = (bf16[32,2,16,4]{3,2,0,1:T(8,128)(2,1)S(1)}, bf16[32,2,16,4]{3,2,0,1:T(8,128)(2,1)S(1)}, u32[]{:S(2)}, u32[]{:S(2)}) collective-permute-start(bf16[32,2,16,4]{3,2,0,1:T(8,128)(2,1)S(1)} %get-tuple-element.11), channel_id=1, source_target_pairs={{0,8},{8,16},{16,24},{1,9},{9,17},{17,25},{2,10},{10,18},{18,26},{... | collective-permute-start | bytes 24584 | tf_op jit(solution)/shard_map/ppermute | solution.py:14
  99.6 6.5 %collective-permute-done = bf16[32,2,16,4]{3,2,0,1:T(8,128)(2,1)S(1)} collective-permute-done((bf16[32,2,16,4]{3,2,0,1:T(8,128)(2,1)S(1)}, bf16[32,2,16,4]{3,2,0,1:T(8,128)(2,1)S(1)}, u32[]{:S(2)}, u32[]{:S(2)}) %collective-permute-start) | collective-permute-done | bytes 8224 | tf_op jit(solution)/shard_map/ppermute | solution.py:14
  106.1 4.8 %concatenate.9 = bf16[32,2,16,1032]{3,2,0,1:T(8,128)(2,1)S(1)} concatenate(bf16[32,2,16,4]{3,2,0,1:T(8,128)(2,1)S(1)} %collective-permute-done, bf16[32,2,16,1024]{3,2,0,1:T(8,128)(2,1)} %copy.45, bf16[32,2,16,4]{3,2,0,1:T(8,128)(2,1)S(1)} %collective-permute-done.1), dimensions={3} | concatenate | bytes 4227072 | tf_op jit(solution)/shard_map/concatenate | solution.py:18
  111.4 6.8 %collective-permute-start.2 = (bf16[32,2,4,1032]{3,2,0,1:T(4,128)(2,1)S(1)}, bf16[32,2,4,1032]{3,2,0,1:T(4,128)(2,1)S(1)}, u32[]{:S(2)}, u32[]{:S(2)}) collective-permute-start(bf16[32,2,4,1032]{3,2,0,1:T(4,128)(2,1)S(1)} %get-tuple-element.8), channel_id=1, source_target_pairs={{0,1},{1,2},{2,3},{3,4},{4,5},{5,6},{6,7},{8,9},{9,10},{10,11},{11... | collective-permute-start | bytes 1585160 | tf_op jit(solution)/shard_map/ppermute | solution.py:14
  118.2 2.1 %collective-permute-start.3 = (bf16[32,2,4,1032]{3,2,0,1:T(4,128)(2,1)S(1)}, bf16[32,2,4,1032]{3,2,0,1:T(4,128)(2,1)S(1)}, u32[]{:S(2)}, u32[]{:S(2)}) collective-permute-start(bf16[32,2,4,1032]{3,2,0,1:T(4,128)(2,1)S(1)} %get-tuple-element.9), channel_id=1, source_target_pairs={{1,0},{2,1},{3,2},{4,3},{5,4},{6,5},{7,6},{9,8},{10,9},{11,10},{12... | collective-permute-start | bytes 1585160 | tf_op jit(solution)/shard_map/ppermute | solution.py:17
  120.3 4.7 %collective-permute-done.2 = bf16[32,2,4,1032]{3,2,0,1:T(4,128)(2,1)S(1)} collective-permute-done((bf16[32,2,4,1032]{3,2,0,1:T(4,128)(2,1)S(1)}, bf16[32,2,4,1032]{3,2,0,1:T(4,128)(2,1)S(1)}, u32[]{:S(2)}, u32[]{:S(2)}) %collective-permute-start.2) | collective-permute-done | bytes 528416 | tf_op jit(solution)/shard_map/ppermute | solution.py:14
  125.0 4.4 %collective-permute-done.3 = bf16[32,2,4,1032]{3,2,0,1:T(4,128)(2,1)S(1)} collective-permute-done((bf16[32,2,4,1032]{3,2,0,1:T(4,128)(2,1)S(1)}, bf16[32,2,4,1032]{3,2,0,1:T(4,128)(2,1)S(1)}, u32[]{:S(2)}, u32[]{:S(2)}) %collective-permute-start.3) | collective-permute-done | bytes 528416 | tf_op jit(solution)/shard_map/ppermute | solution.py:17
  131.1 2.1 %fusion.16 = f32[32,24,1032]{2,1,0:T(8,128)} fusion(f32[32,2,24,1032]{3,2,0,1:T(8,128)S(1)} %maximum_convert_fusion), kind=kLoop, calls=%fused_computation.23 | loop fusion | flops 2377728 | bytes 9510912 | tf_op jit(solution)/shard_map/add | solution.py:39
  133.2 3.4 %copy.48 = f32[32,2,24,1032]{3,2,1,0:T(8,128)} copy(f32[32,2,24,1032]{3,2,0,1:T(8,128)S(1)} %maximum_convert_fusion) | data formatting | bytes 12681216 | tf_op jit(solution)/shard_map/convert_element_type | solution.py:38
  136.6 6.9 %gather_fusion.1 = f32[32,2,24,1032]{3,2,1,0:T(8,128)} fusion(f32[32,2,24,1032]{3,2,1,0:T(8,128)} %copy.48, s32[1024]{0:T(1024)S(1)} %pad_clamp_fusion), kind=kCustom, calls=%fused_computation.2.clone | custom fusion | bytes 12681344 | tf_op jit(solution)/shard_map/jit(_take)/gather | solution.py:41
  143.5 6.8 %gather_fusion = f32[32,2,24,1032]{3,2,1,0:T(8,128)} fusion(f32[32,2,24,1032]{3,2,1,0:T(8,128)} %copy.48, s32[1024]{0:T(1024)S(1)} %pad_clamp_fusion.1), kind=kCustom, calls=%fused_computation.clone | custom fusion | bytes 12681344 | tf_op jit(solution)/shard_map/jit(_take)/gather | solution.py:40
  150.3 5.7 %copy_select_fusion = (f32[32,2,24,1032]{3,2,0,1:T(8,128)S(1)}, f32[32,2,24,1032]{3,2,0,1:T(8,128)S(1)}) fusion(f32[32,2,24,1032]{3,2,1,0:T(8,128)} %gather_fusion.1, pred[32]{0:T(512)(128)(4,1)S(1)} %compare_and_fusion, f32[32,2,24,1032]{3,2,1,0:T(8,128)} %gather_fusion, pred[32]{0:T(512)(128)(4,1)S(1)} %compare_and_fusion.1), kind=kLoop, calls=%fused_computation.13 | loop fusion | flops 3170304 | bytes 25362496 | tf_op jit(solution)/shard_map/jit(_take)/select_n | solution.py:41
  156.1 3.6 %add_bitcast_fusion = (f32[32,24,1032]{2,1,0:T(8,128)}, f32[32,24,1032]{2,1,0:T(8,128)}) fusion(f32[32,2,24,1032]{3,2,0,1:T(8,128)S(1)} %get-tuple-element.18, f32[32,2,24,1032]{3,2,0,1:T(8,128)S(1)} %get-tuple-element.19), kind=kLoop, calls=%fused_computation.27 | loop fusion | flops 4755456 | bytes 19021824 | tf_op jit(solution)/shard_map/add | solution.py:42
  159.7 9.5 %fusion = f32[96,1032,16]{1,2,0:T(8,128)S(1)} fusion(f32[32,24,1032]{2,1,0:T(8,128)} %get-tuple-element.5, f32[32,24,1032]{2,1,0:T(8,128)} %get-tuple-element.4, f32[32,24,1032]{2,1,0:T(8,128)} %fusion.16), kind=kOutput, calls=%fused_computation.5 | convolution fusion | flops 461281152 | bytes 15851520 | tf_op jit(solution)/shard_map/ij,fjw->fiw/dot_general | solution.py:32
  169.2 26.8 %broadcast_multiply_fusion = f32[96,16,1024]{2,1,0:T(8,128)S(1)} fusion(f32[96,1032,16]{1,2,0:T(8,128)S(1)} %fusion), kind=kOutput, calls=%fused_computation.28 | convolution fusion | flops 19485204480 | bytes 12632064 | tf_op jit(solution)/shard_map/fiw,wk->fik/dot_general | solution.py:33
  196.1 2.7 %copy-done = f32[96,16,1024]{2,1,0:T(8,128)} copy-done((f32[96,16,1024]{2,1,0:T(8,128)}, f32[96,16,1024]{2,1,0:T(8,128)S(1)}, u32[]{:S(2)}) %copy-start) | copy-done | bytes 6291480
  202.9 7.1 %divide_log_fusion = (f32[32,16,1024]{2,1,0:T(8,128)}, f32[32,16,1024]{2,1,0:T(8,128)}) fusion(f32[32,16,1024]{2,1,0:T(8,128)} %gather_fusion.3, f32[32,16,1024]{2,1,0:T(8,128)} %gather_fusion.2, pred[32]{0:T(512)(128)(4,1)S(1)} %compare_and_fusion, pred[32]{0:T(512)(128)(4,1)S(1)} %compare_and_fusion.1, f32[96,16,1024]{2,1,0:T(8,128)} %copy-done), kind=kLoop, calls=%fused_computation.41 | loop fusion | flops 4194304 | bytes 12582976 | tf_op jit(solution)/shard_map/log | solution.py:56
  (33 shorter events, 15.2 us)
Async XLA Ops:
  59.4 5.5 %copy-start.1 = (bf16[32,32]{1,0:T(8,128)(2,1)S(1)}, bf16[32,32]{1,0:T(8,128)(2,1)}, u32[]{:S(2)}) copy-start(bf16[32,32]{1,0:T(8,128)(2,1)} %param.11) | copy-start | bytes 6148
  59.4 5.5 %copy-start.2 = (bf16[32,32]{1,0:T(8,128)(2,1)S(1)}, bf16[32,32]{1,0:T(8,128)(2,1)}, u32[]{:S(2)}) copy-start(bf16[32,32]{1,0:T(8,128)(2,1)} %param.10) | copy-start | bytes 6148
  61.0 5.3 %copy-start.3 = (s32[32]{0:T(128)S(1)}, s32[32]{0:T(128)}, u32[]{:S(2)}) copy-start(s32[32]{0:T(128)} %param.12) | copy-start | bytes 388
  61.0 5.3 %copy-start.4 = (s32[32]{0:T(128)S(1)}, s32[32]{0:T(128)}, u32[]{:S(2)}) copy-start(s32[32]{0:T(128)} %param.13) | copy-start | bytes 388
  61.0 27.5 %all-to-all-start.1 = ((bf16[4,8,2,16,1024]{4,3,2,1,0:T(8,128)(2,1)}), bf16[4,8,2,16,1024]{4,3,2,1,0:T(8,128)(2,1)S(1)}, u32[]{:S(2)}, u32[]{:S(2)}) async-start(bf16[4,8,2,16,1024]{4,3,2,1,0:T(8,128)(2,1)} %pad_maximum_fusion), calls=%async_computation.1 | async-start | bytes 4194304 | tf_op jit(solution)/shard_map/all_to_all | solution.py:70
  91.9 7.8 %collective-permute-start.1 = (bf16[32,2,16,4]{3,2,0,1:T(8,128)(2,1)S(1)}, bf16[32,2,16,4]{3,2,0,1:T(8,128)(2,1)S(1)}, u32[]{:S(2)}, u32[]{:S(2)}) collective-permute-start(bf16[32,2,16,4]{3,2,0,1:T(8,128)(2,1)S(1)} %get-tuple-element.10), channel_id=1, source_target_pairs={{8,0},{16,8},{24,16},{9,1},{17,9},{25,17},{10,2},{18,10},{26,18},{... | collective-permute-start | bytes 24584 | tf_op jit(solution)/shard_map/ppermute | solution.py:17
  94.9 11.2 %collective-permute-start = (bf16[32,2,16,4]{3,2,0,1:T(8,128)(2,1)S(1)}, bf16[32,2,16,4]{3,2,0,1:T(8,128)(2,1)S(1)}, u32[]{:S(2)}, u32[]{:S(2)}) collective-permute-start(bf16[32,2,16,4]{3,2,0,1:T(8,128)(2,1)S(1)} %get-tuple-element.11), channel_id=1, source_target_pairs={{0,8},{8,16},{16,24},{1,9},{9,17},{17,25},{2,10},{10,18},{18,26},{... | collective-permute-start | bytes 24584 | tf_op jit(solution)/shard_map/ppermute | solution.py:14
  111.4 13.6 %collective-permute-start.2 = (bf16[32,2,4,1032]{3,2,0,1:T(4,128)(2,1)S(1)}, bf16[32,2,4,1032]{3,2,0,1:T(4,128)(2,1)S(1)}, u32[]{:S(2)}, u32[]{:S(2)}) collective-permute-start(bf16[32,2,4,1032]{3,2,0,1:T(4,128)(2,1)S(1)} %get-tuple-element.8), channel_id=1, source_target_pairs={{0,1},{1,2},{2,3},{3,4},{4,5},{5,6},{6,7},{8,9},{9,10},{10,11},{11... | collective-permute-start | bytes 1585160 | tf_op jit(solution)/shard_map/ppermute | solution.py:14
  118.2 11.2 %collective-permute-start.3 = (bf16[32,2,4,1032]{3,2,0,1:T(4,128)(2,1)S(1)}, bf16[32,2,4,1032]{3,2,0,1:T(4,128)(2,1)S(1)}, u32[]{:S(2)}, u32[]{:S(2)}) collective-permute-start(bf16[32,2,4,1032]{3,2,0,1:T(4,128)(2,1)S(1)} %get-tuple-element.9), channel_id=1, source_target_pairs={{1,0},{2,1},{3,2},{4,3},{5,4},{6,5},{7,6},{9,8},{10,9},{11,10},{12... | collective-permute-start | bytes 1585160 | tf_op jit(solution)/shard_map/ppermute | solution.py:17
  196.1 2.7 %copy-start = (f32[96,16,1024]{2,1,0:T(8,128)}, f32[96,16,1024]{2,1,0:T(8,128)S(1)}, u32[]{:S(2)}) copy-start(f32[96,16,1024]{2,1,0:T(8,128)S(1)} %broadcast_multiply_fusion) | copy-start | bytes 18874372
